TPU v7x, 256 devices: a whole 4x4x8 slice. The times are simulated.
256 devices in a mesh: section: 8 (over x, core), dp: 32 (over y, z).
Axes of the slice: x: 4, y: 4, z: 8, core: 2. Of those that a mesh axis runs over, the one named last changes fastest.
Arguments:
- resid_in: bfloat16 [4, 1024, 2048], P(None, 'dp'), may hold values from -10 to 10
- dest_row: int32 [4, 1024], replicated, may hold values from 0 to 1023, as said below
- doc_ids: int32 [4, 1024], P(None, 'dp'), may hold values from 0 to 1023, as said below
- cotangent: bfloat16 [4, 1024, 2048], P(None, 'dp'), may hold values from -0.119628906 to 0.119628906
- gain: float32 [8, 2048], P('section'), may hold values from 0.5 to 1.5
- steer: float32 [8, 2048], P('section'), may hold values from -3 to 3
- w_query: bfloat16 [8, 2048, 1024], P('section', 'dp'), may hold values from -1 to 1
- w_keyval: bfloat16 [8, 2048, 512], P('section', 'dp'), may hold values from -1 to 1
- w_out: bfloat16 [8, 1024, 2048], P('section', None, 'dp'), may hold values from -0.1875 to 0.1875
Outputs:
- hidden_out: bfloat16 [8, 4, 1024, 2048], P('section', None, 'dp')
- grad_steer: float32 [8, 2048], P('section')
Inputs may be any that keep to these rules, and one draw needn't show every extreme that they name: Each row of dest_row is a permutation of 0 to 1023. Counting the tokens of one aligned block of 32 input tokens that go to one aligned block of 32 packed rows, no count exceeds 2, and some reach it in every micro-batch. doc_ids never falls along a row; every value is a row index r at which doc_ids equals r; each aligned block of 32 rows begins a document, so no document crosses such a block.
All inputs are finite; a program needn't handle non-finite values.
Results may differ from a plain program's by a relative error of at most 0.02.
Values may be sent and summed in bfloat16 or wider, within the bound.
No kernel may reach another device: no remote copies, remote signals or barrier semaphores. Data moves between devices by JAX's collectives and lax.ppermute only.
A program may use at most 64 MiB of HBM per device.

v0:
```python
import jax
import jax.numpy as jnp
from jax import lax
from jax.sharding import PartitionSpec as P

HD = 64
ROPE_BASE = 500000.0
EPSILON = 1e-05
MASKED = -1e30


def rotate(values, positions):
    half_size = values.shape[-1] // 2
    freq_index = jnp.arange(half_size, dtype=jnp.float32)
    inverse = ROPE_BASE ** (-2.0 * freq_index / values.shape[-1])
    angles = positions.astype(jnp.float32)[..., None] * inverse
    cosine = jnp.cos(angles)[..., None, :]
    sine_part = jnp.sin(angles)[..., None, :]
    first_half = values[..., :half_size]
    second = values[..., half_size:]
    return jnp.concatenate(
        [first_half * cosine - second * sine_part, second * cosine + first_half * sine_part],
        axis=-1,
    )


def layer(hidden_in, steering, gain_row, w_query, w_keyval, w_out, positions, documents):
    micro_count, row_count, width = hidden_in.shape
    head_size = HD
    kv_heads = w_keyval.shape[1] // (2 * head_size)
    query_heads = w_query.shape[1] // head_size
    group_size = query_heads // kv_heads
    residual = hidden_in.astype(jnp.float32) + steering
    normed = (
        residual
        * lax.rsqrt(jnp.mean(residual * residual, axis=-1, keepdims=True) + EPSILON)
        * gain_row
    ).astype(jnp.bfloat16)
    flat = normed.reshape(micro_count * row_count, width)
    queries = jnp.dot(flat, w_query, preferred_element_type=jnp.float32).reshape(
        micro_count, row_count, query_heads, head_size
    )
    keyval = jnp.dot(flat, w_keyval, preferred_element_type=jnp.float32).reshape(
        micro_count, row_count, 2 * kv_heads * head_size
    )
    key_rows = rotate(
        keyval[..., : kv_heads * head_size].reshape(micro_count, row_count, kv_heads, head_size),
        positions,
    ).astype(jnp.bfloat16)
    values = (
        keyval[..., kv_heads * head_size :]
        .reshape(micro_count, row_count, kv_heads, head_size)
        .astype(jnp.bfloat16)
    )
    queries = (
        rotate(queries, positions)
        .astype(jnp.bfloat16)
        .reshape(micro_count, row_count, kv_heads, group_size, head_size)
    )
    scores = jnp.einsum(
        "mrkgd,mskd->mkgrs", queries, key_rows, preferred_element_type=jnp.float32
    ) * head_size ** (-0.5)
    row_index = jnp.arange(row_count)
    allowed = (documents[:, :, None] == documents[:, None, :]) & (
        row_index[:, None] >= row_index[None, :]
    )
    scores = jnp.where(allowed[:, None, None], scores, MASKED)
    peak = jnp.max(scores, axis=-1, keepdims=True)
    weights = jnp.exp(scores - peak)
    weights = (weights / jnp.sum(weights, axis=-1, keepdims=True)).astype(jnp.bfloat16)
    mixed_heads = jnp.einsum(
        "mkgrs,mskd->mrkgd", weights, values, preferred_element_type=jnp.float32
    ).astype(jnp.bfloat16)
    mixed_heads = mixed_heads.reshape(micro_count * row_count, query_heads * head_size)
    projected = jnp.dot(mixed_heads, w_out, preferred_element_type=jnp.float32).reshape(
        micro_count, row_count, width
    )
    return (residual + projected).astype(jnp.bfloat16)


def plan_slots(target, device, row_count, capacity, dp_count):
    target_grid = target.reshape(dp_count, row_count)
    target_dev = target_grid // row_count
    target_off = target_grid % row_count
    row_order = jnp.arange(row_count, dtype=jnp.int32)
    matching = target_dev[:, :, None] == target_dev[:, None, :]
    earlier = row_order[None, :] < row_order[:, None]
    rank_ids = jnp.sum((matching & earlier[None]).astype(jnp.int32), axis=2)
    slot_ids = target_dev * capacity + rank_ids
    own_slot = lax.dynamic_index_in_dim(slot_ids, device, 0, keepdims=False)
    column_ids = jnp.arange(dp_count, dtype=jnp.int32)[:, None] * capacity + rank_ids
    landing = (target_dev == device)[None] & (target_off[None] == row_order[:, None, None])
    source_col = jnp.sum(jnp.where(landing, column_ids[None], 0), axis=(1, 2))
    return (own_slot, source_col)


def pack_rows(source_rows, own_slot, slot_count):
    selector = (jnp.arange(slot_count, dtype=jnp.int32)[:, None] == own_slot[None, :]).astype(
        jnp.bfloat16
    )
    return jnp.dot(selector, source_rows, preferred_element_type=jnp.float32).astype(jnp.bfloat16)


def unpack_rows(arrived, source_col):
    selector = (
        source_col[:, None] == jnp.arange(arrived.shape[0], dtype=jnp.int32)[None, :]
    ).astype(jnp.bfloat16)
    return jnp.dot(selector, arrived, preferred_element_type=jnp.float32).astype(jnp.bfloat16)


def body(resid_in, dest_row, doc_ids, cotangent, gain, steer, w_query, w_keyval, w_out):
    dp_count = lax.axis_size("dp")
    section_count = lax.axis_size("section")
    device = lax.axis_index("dp")
    section_idx = lax.axis_index("section")
    micro_count, row_count, width = resid_in.shape
    capacity = row_count // dp_count + 1
    slot_count = dp_count * capacity
    full_query, full_keyval, full_out = (
        lax.all_gather(w_query[0], "dp", axis=0, tiled=True),
        lax.all_gather(w_keyval[0], "dp", axis=0, tiled=True),
        lax.all_gather(w_out[0], "dp", axis=1, tiled=True),
    )
    gain_row = gain[0]
    steering = steer[0]
    plans = [
        plan_slots(dest_row[micro_idx], device, row_count, capacity, dp_count)
        for micro_idx in range(micro_count)
    ]
    packed = jnp.stack(
        [
            pack_rows(resid_in[micro_idx], plans[micro_idx][0], slot_count).reshape(
                dp_count, capacity, width
            )
            for micro_idx in range(micro_count)
        ],
        axis=1,
    )
    arrived = lax.all_to_all(packed, "dp", split_axis=0, concat_axis=0, tiled=True)
    grouped = jnp.stack(
        [
            unpack_rows(arrived[:, micro_idx].reshape(slot_count, width), plans[micro_idx][1])
            for micro_idx in range(micro_count)
        ]
    )
    global_rows = device * row_count + jnp.arange(row_count, dtype=jnp.int32)
    positions = global_rows[None, :] - doc_ids

    def run_layer(hidden_in, steer_vec):
        return layer(
            hidden_in, steer_vec, gain_row, full_query, full_keyval, full_out, positions, doc_ids
        )

    zero_block = jnp.zeros((micro_count, row_count, width), jnp.bfloat16)
    forward_route = [(i, i + 1) for i in range(section_count - 1)]
    backward_route = [(i + 1, i) for i in range(section_count - 1)]

    def forward_step(carry, step):
        incoming, kept, produced = carry
        active = section_idx == step
        hidden_in = jnp.where(step == 0, grouped, incoming)
        kept = jnp.where(active, hidden_in, kept)
        hidden_new = lax.cond(active, lambda: run_layer(hidden_in, steering), lambda: zero_block)
        produced = jnp.where(active, hidden_new, produced)
        sent = lax.ppermute(hidden_new, "section", forward_route)
        return ((sent, kept, produced), None)

    (unused_in, kept, produced), unused_ys = lax.scan(
        forward_step,
        (zero_block, zero_block, zero_block),
        jnp.arange(section_count, dtype=jnp.int32),
    )

    def backward_step(carry, step):
        incoming, grad_sum = carry
        active = section_idx == step
        upstream = jnp.where(step == section_count - 1, cotangent, incoming)

        def differentiate():
            unused_out, pullback = jax.vjp(run_layer, kept, steering)
            return pullback(upstream)

        grad_in, steer_part = lax.cond(
            active, differentiate, lambda: (zero_block, jnp.zeros_like(steering))
        )
        sent = lax.ppermute(grad_in, "section", backward_route)
        return ((sent, grad_sum + steer_part), None)

    (unused_grad, grad_sum), unused_zs = lax.scan(
        backward_step,
        (zero_block, jnp.zeros_like(steering)),
        jnp.arange(section_count - 1, -1, -1, dtype=jnp.int32),
    )
    total = lax.psum(grad_sum, "dp")
    return (produced[None], total[None])


def solution(mesh):
    in_specs = (
        P(None, "dp", None),
        P(),
        P(None, "dp"),
        P(None, "dp", None),
        P("section", None),
        P("section", None),
        P("section", "dp", None),
        P("section", "dp", None),
        P("section", None, "dp"),
    )
    out_specs = (P("section", None, "dp", None), P("section", None))
    return jax.shard_map(body, mesh=mesh, in_specs=in_specs, out_specs=out_specs, check_vma=False)
```

profile of v0, /device:TPU:0, one launch (start us, length us, event | category | flops | bytes accessed | tf_op | source)
XLA Modules:
  0.0 964.3 jit_solution(17783899758612930752)
XLA Ops:
  21.3 10.0 %all-to-all-start = ((bf16[32,4,2,2048]{3,2,1,0:T(2,128)(2,1)}), bf16[32,4,2,2048]{3,2,1,0:T(2,128)(2,1)S(1)}, u32[]{:S(2)}, u32[]{:S(2)}) async-start(bf16[32,4,2,2048]{3,2,1,0:T(2,128)(2,1)} %pad_maximum_fusion.3), calls=%async_computation | async-start | bytes 2097152 | tf_op jit(solution)/shard_map/all_to_all | solution.py:139
  36.0 26.9 %all-to-all-done = bf16[32,4,2,2048]{3,2,1,0:T(2,128)(2,1)S(1)} async-done(((bf16[32,4,2,2048]{3,2,1,0:T(2,128)(2,1)}), bf16[32,4,2,2048]{3,2,1,0:T(2,128)(2,1)S(1)}, u32[]{:S(2)}, u32[]{:S(2)}) %all-to-all-start) | async-done | bytes 1048608 | tf_op jit(solution)/shard_map/all_to_all | solution.py:139
  65.2 32.7 %all-gather.9.cloned.1.call-done = bf16[1,2048,1024]{2,1,0:T(8,128)(2,1)} async-done(((bf16[1,64,1024]{2,1,0:T(8,128)(2,1)}), bf16[1,2048,1024]{2,1,0:T(8,128)(2,1)}) %all-gather.9.cloned.1.call-update) | async-done | bytes 4194320 | tf_op jit(solution)/shard_map/all_gather | solution.py:120
  104.4 74.7 %all-gather.11.cloned.1.call-done = bf16[1,1024,2048]{1,2,0:T(8,128)(2,1)} async-done(((bf16[1,1024,64]{1,2,0:T(8,128)(2,1)}), bf16[1,1024,2048]{1,2,0:T(8,128)(2,1)}) %all-gather.11.cloned.1.call-update) | async-done | bytes 4194320 | tf_op jit(solution)/shard_map/all_gather | solution.py:122
  179.1 6.5 copy.80
  185.6 71.0 %all-gather.7.cloned.1.call-done = bf16[1,2048,512]{2,1,0:T(8,128)(2,1)} async-done(((bf16[1,64,512]{2,1,0:T(8,128)(2,1)}), bf16[1,2048,512]{2,1,0:T(8,128)(2,1)}) %all-gather.7.cloned.1.call-update) | async-done | bytes 2097168 | tf_op jit(solution)/shard_map/all_gather | solution.py:121
  256.7 157.6 %while.28 = (s32[]{:T(128)}, bf16[4,32,2048]{2,1,0:T(8,128)(2,1)S(1)}, bf16[4,32,2048]{2,1,0:T(8,128)(2,1)S(1)}, bf16[4,32,2048]{2,1,0:T(8,128)(2,1)}, s32[8]{0:...) while((s32[]{:T(128)}, ...), condition=%wide.region_14.15_spmd.clone, body=%wide.region_8.14_spmd.clone.sunk | while | flops 1376075008 | bytes 24693816 | solution.py:168
  258.7 18.0 %conditional.6 = (bf16[4,32,2048]{2,1,0:T(8,128)(2,1)S(1)}) conditional(s32[]{:T(128)} %convert_element_type.335, () %tuple.113, (bf16[4,32,2048]{2,1,0:T(8,128)(2,1)S(1)}, f32[1,2048]{1,0:T(1,128)}, f32[1,2048]{1,0:T(1,128)}, bf16[2048,512]{1,0:T(8,128)(2,1)}, s32[4,32]{1,0:T(4,128)}, /*index=5*/s32[4,32]{1,0:T(4,128)}, ...), branch_computations={%region_9.9_spmd, %region_10.13_spmd} | conditional | flops 1374764288 | bytes 18402056 | solution.py:163
  281.5 20.2 %collective-permute-start = (bf16[4,32,2048]{2,1,0:T(8,128)(2,1)S(1)}, bf16[4,32,2048]{2,1,0:T(8,128)(2,1)S(1)}, u32[]{:S(2)}, u32[]{:S(2)}) collective-permute-start(bf16[4,32,2048]{2,1,0:T(8,128)(2,1)S(1)} %get-tuple-element.784), channel_id=1, source_target_pairs={{0,32},{32,64},{64,96},{96,128},{128,160},{160,192},{192,224},{1,3... | collective-permute-start | bytes 1572872 | tf_op jit(solution)/shard_map/while/body/eval_jaxpr/ppermute | solution.py:165
  315.8 26.5 %collective-permute-start = (bf16[4,32,2048]{2,1,0:T(8,128)(2,1)S(1)}, bf16[4,32,2048]{2,1,0:T(8,128)(2,1)S(1)}, u32[]{:S(2)}, u32[]{:S(2)}) collective-permute-start(bf16[4,32,2048]{2,1,0:T(8,128)(2,1)S(1)} %get-tuple-element.784), channel_id=1, source_target_pairs={{0,32},{32,64},{64,96},{96,128},{128,160},{160,192},{192,224},{1,3... | collective-permute-start | bytes 1572872 | tf_op jit(solution)/shard_map/while/body/eval_jaxpr/ppermute | solution.py:165
  346.2 8.6 collective-permute-start
  358.7 13.1 %collective-permute-start = (bf16[4,32,2048]{2,1,0:T(8,128)(2,1)S(1)}, bf16[4,32,2048]{2,1,0:T(8,128)(2,1)S(1)}, u32[]{:S(2)}, u32[]{:S(2)}) collective-permute-start(bf16[4,32,2048]{2,1,0:T(8,128)(2,1)S(1)} %get-tuple-element.784), channel_id=1, source_target_pairs={{0,32},{32,64},{64,96},{96,128},{128,160},{160,192},{192,224},{1,3... | collective-permute-start | bytes 1572872 | tf_op jit(solution)/shard_map/while/body/eval_jaxpr/ppermute | solution.py:165
  375.8 8.6 collective-permute-start
  388.3 24.0 %collective-permute-start = (bf16[4,32,2048]{2,1,0:T(8,128)(2,1)S(1)}, bf16[4,32,2048]{2,1,0:T(8,128)(2,1)S(1)}, u32[]{:S(2)}, u32[]{:S(2)}) collective-permute-start(bf16[4,32,2048]{2,1,0:T(8,128)(2,1)S(1)} %get-tuple-element.784), channel_id=1, source_target_pairs={{0,32},{32,64},{64,96},{96,128},{128,160},{160,192},{192,224},{1,3... | collective-permute-start | bytes 1572872 | tf_op jit(solution)/shard_map/while/body/eval_jaxpr/ppermute | solution.py:165
  415.2 469.1 %while.29 = (s32[]{:T(128)}, bf16[4,32,2048]{2,1,0:T(8,128)(2,1)}, f32[2048]{0:T(1024)}, s32[8]{0:T(128)}, s32[]{:T(128)}, /*index=5*/bf16[4,32,2048]{2,1,0:T(8,...) while((s32[]{:T(128)}, bf16[4,32,2048]{2,1,0:T(8,128)(2,1)}, ...), condition=%wide.region_26.27_spmd.clone, body=%wide.region_15.26_spmd.clone.sunk | while | flops 2205098752 | bytes 54051516 | solution.py:189
  421.3 7.6 collective-permute-done.1
  435.8 13.3 %collective-permute-done.1 = bf16[4,32,2048]{2,1,0:T(8,128)(2,1)S(1)} collective-permute-done((bf16[4,32,2048]{2,1,0:T(8,128)(2,1)}, bf16[4,32,2048]{2,1,0:T(8,128)(2,1)S(1)}, u32[]{:S(2)}, u32[]{:S(2)}) %collective-permute-start.1) | collective-permute-done | bytes 524320 | tf_op jit(solution)/shard_map/while/body/eval_jaxpr/ppermute | solution.py:186
  456.2 8.1 collective-permute-done.1
  471.2 23.7 %collective-permute-done.1 = bf16[4,32,2048]{2,1,0:T(8,128)(2,1)S(1)} collective-permute-done((bf16[4,32,2048]{2,1,0:T(8,128)(2,1)}, bf16[4,32,2048]{2,1,0:T(8,128)(2,1)S(1)}, u32[]{:S(2)}, u32[]{:S(2)}) %collective-permute-start.1) | collective-permute-done | bytes 524320 | tf_op jit(solution)/shard_map/while/body/eval_jaxpr/ppermute | solution.py:186
  502.0 8.1 collective-permute-done.1
  517.0 12.8 %collective-permute-done.1 = bf16[4,32,2048]{2,1,0:T(8,128)(2,1)S(1)} collective-permute-done((bf16[4,32,2048]{2,1,0:T(8,128)(2,1)}, bf16[4,32,2048]{2,1,0:T(8,128)(2,1)S(1)}, u32[]{:S(2)}, u32[]{:S(2)}) %collective-permute-start.1) | collective-permute-done | bytes 524320 | tf_op jit(solution)/shard_map/while/body/eval_jaxpr/ppermute | solution.py:186
  536.9 295.9 %collective-permute-done.1 = bf16[4,32,2048]{2,1,0:T(8,128)(2,1)S(1)} collective-permute-done((bf16[4,32,2048]{2,1,0:T(8,128)(2,1)}, bf16[4,32,2048]{2,1,0:T(8,128)(2,1)S(1)}, u32[]{:S(2)}, u32[]{:S(2)}) %collective-permute-start.1) | collective-permute-done | bytes 524320 | tf_op jit(solution)/shard_map/while/body/eval_jaxpr/ppermute | solution.py:186
  835.7 43.7 %conditional.7 = (bf16[4,32,2048]{2,1,0:T(8,128)(2,1)}, f32[2048]{0:T(1024)}) conditional(s32[]{:T(128)} %convert_element_type.336, () %tuple.116, (s32[]{:T(128)}, bf16[4,32,2048]{2,1,0:T(8,128)(2,1)}, bf16[4,32,2048]{2,1,0:T(8,128)(2,1)}, bf16[1024,2048]{1,0:T(8,128)(2,1)}, s32[4,32]{1,0:T(4,128)}, ...), branch_computations={%region_16.16_spmd, %region_17.25_spmd} | conditional | flops 2205094656 | bytes 49832296 | solution.py:183
  884.3 73.4 %psum.7 = f32[1,2048]{1,0:T(1,128)} all-reduce(f32[1,2048]{1,0:T(1,128)} %bitcast.243), channel_id=1, replica_groups=mesh['section'=8,'dp'=32] {'dp'}, use_global_device_ids=true, to_apply=%region_27.28 | all-reduce | flops 2048 | bytes 16384 | tf_op jit(solution)/shard_map/psum | solution.py:194
  (277 shorter events, 179.3 us)
Async XLA Ops:
  7.2 90.8 %all-gather.9.cloned.1.call-start = ((), (), s32[]{:S(2)}) async-start(), calls=%async_computation.2 | async-start | bytes 4325376 | tf_op jit(solution)/shard_map/all_gather | solution.py:120
  7.9 171.2 %all-gather.11.cloned.1.call-start = ((), (), s32[]{:S(2)}) async-start(), calls=%async_computation.3 | async-start | bytes 4325376 | tf_op jit(solution)/shard_map/all_gather | solution.py:122
  8.6 248.0 %all-gather.7.cloned.1.call-start = ((), (), s32[]{:S(2)}) async-start(), calls=%async_computation.1 | async-start | bytes 2162688 | tf_op jit(solution)/shard_map/all_gather | solution.py:121
  21.3 41.6 %all-to-all-start = ((bf16[32,4,2,2048]{3,2,1,0:T(2,128)(2,1)}), bf16[32,4,2,2048]{3,2,1,0:T(2,128)(2,1)S(1)}, u32[]{:S(2)}, u32[]{:S(2)}) async-start(bf16[32,4,2,2048]{3,2,1,0:T(2,128)(2,1)} %pad_maximum_fusion.3), calls=%async_computation | async-start | bytes 2097152 | tf_op jit(solution)/shard_map/all_to_all | solution.py:139
  276.6 2.8 collective-permute-start
  281.5 22.1 %collective-permute-start = (bf16[4,32,2048]{2,1,0:T(8,128)(2,1)S(1)}, bf16[4,32,2048]{2,1,0:T(8,128)(2,1)S(1)}, u32[]{:S(2)}, u32[]{:S(2)}) collective-permute-start(bf16[4,32,2048]{2,1,0:T(8,128)(2,1)S(1)} %get-tuple-element.784), channel_id=1, source_target_pairs={{0,32},{32,64},{64,96},{96,128},{128,160},{160,192},{192,224},{1,3... | collective-permute-start | bytes 1572872 | tf_op jit(solution)/shard_map/while/body/eval_jaxpr/ppermute | solution.py:165
  305.7 8.0 collective-permute-start
  315.8 28.4 %collective-permute-start = (bf16[4,32,2048]{2,1,0:T(8,128)(2,1)S(1)}, bf16[4,32,2048]{2,1,0:T(8,128)(2,1)S(1)}, u32[]{:S(2)}, u32[]{:S(2)}) collective-permute-start(bf16[4,32,2048]{2,1,0:T(8,128)(2,1)S(1)} %get-tuple-element.784), channel_id=1, source_target_pairs={{0,32},{32,64},{64,96},{96,128},{128,160},{160,192},{192,224},{1,3... | collective-permute-start | bytes 1572872 | tf_op jit(solution)/shard_map/while/body/eval_jaxpr/ppermute | solution.py:165
  346.2 10.5 %collective-permute-start = (bf16[4,32,2048]{2,1,0:T(8,128)(2,1)S(1)}, bf16[4,32,2048]{2,1,0:T(8,128)(2,1)S(1)}, u32[]{:S(2)}, u32[]{:S(2)}) collective-permute-start(bf16[4,32,2048]{2,1,0:T(8,128)(2,1)S(1)} %get-tuple-element.784), channel_id=1, source_target_pairs={{0,32},{32,64},{64,96},{96,128},{128,160},{160,192},{192,224},{1,3... | collective-permute-start | bytes 1572872 | tf_op jit(solution)/shard_map/while/body/eval_jaxpr/ppermute | solution.py:165
  358.7 15.0 %collective-permute-start = (bf16[4,32,2048]{2,1,0:T(8,128)(2,1)S(1)}, bf16[4,32,2048]{2,1,0:T(8,128)(2,1)S(1)}, u32[]{:S(2)}, u32[]{:S(2)}) collective-permute-start(bf16[4,32,2048]{2,1,0:T(8,128)(2,1)S(1)} %get-tuple-element.784), channel_id=1, source_target_pairs={{0,32},{32,64},{64,96},{96,128},{128,160},{160,192},{192,224},{1,3... | collective-permute-start | bytes 1572872 | tf_op jit(solution)/shard_map/while/body/eval_jaxpr/ppermute | solution.py:165
  375.8 10.5 %collective-permute-start = (bf16[4,32,2048]{2,1,0:T(8,128)(2,1)S(1)}, bf16[4,32,2048]{2,1,0:T(8,128)(2,1)S(1)}, u32[]{:S(2)}, u32[]{:S(2)}) collective-permute-start(bf16[4,32,2048]{2,1,0:T(8,128)(2,1)S(1)} %get-tuple-element.784), channel_id=1, source_target_pairs={{0,32},{32,64},{64,96},{96,128},{128,160},{160,192},{192,224},{1,3... | collective-permute-start | bytes 1572872 | tf_op jit(solution)/shard_map/while/body/eval_jaxpr/ppermute | solution.py:165
  388.3 25.9 %collective-permute-start = (bf16[4,32,2048]{2,1,0:T(8,128)(2,1)S(1)}, bf16[4,32,2048]{2,1,0:T(8,128)(2,1)S(1)}, u32[]{:S(2)}, u32[]{:S(2)}) collective-permute-start(bf16[4,32,2048]{2,1,0:T(8,128)(2,1)S(1)} %get-tuple-element.784), channel_id=1, source_target_pairs={{0,32},{32,64},{64,96},{96,128},{128,160},{160,192},{192,224},{1,3... | collective-permute-start | bytes 1572872 | tf_op jit(solution)/shard_map/while/body/eval_jaxpr/ppermute | solution.py:165
  418.7 10.2 %collective-permute-start.1 = (bf16[4,32,2048]{2,1,0:T(8,128)(2,1)}, bf16[4,32,2048]{2,1,0:T(8,128)(2,1)S(1)}, u32[]{:S(2)}, u32[]{:S(2)}) collective-permute-start(bf16[4,32,2048]{2,1,0:T(8,128)(2,1)} %get-tuple-element.682), channel_id=1, source_target_pairs={{32,0},{64,32},{96,64},{128,96},{160,128},{192,160},{224,192},{33,... | collective-permute-start | bytes 1572872 | tf_op jit(solution)/shard_map/while/body/eval_jaxpr/ppermute | solution.py:186
  433.2 15.9 %collective-permute-start.1 = (bf16[4,32,2048]{2,1,0:T(8,128)(2,1)}, bf16[4,32,2048]{2,1,0:T(8,128)(2,1)S(1)}, u32[]{:S(2)}, u32[]{:S(2)}) collective-permute-start(bf16[4,32,2048]{2,1,0:T(8,128)(2,1)} %get-tuple-element.682), channel_id=1, source_target_pairs={{32,0},{64,32},{96,64},{128,96},{160,128},{192,160},{224,192},{33,... | collective-permute-start | bytes 1572872 | tf_op jit(solution)/shard_map/while/body/eval_jaxpr/ppermute | solution.py:186
  453.6 10.7 %collective-permute-start.1 = (bf16[4,32,2048]{2,1,0:T(8,128)(2,1)}, bf16[4,32,2048]{2,1,0:T(8,128)(2,1)S(1)}, u32[]{:S(2)}, u32[]{:S(2)}) collective-permute-start(bf16[4,32,2048]{2,1,0:T(8,128)(2,1)} %get-tuple-element.682), channel_id=1, source_target_pairs={{32,0},{64,32},{96,64},{128,96},{160,128},{192,160},{224,192},{33,... | collective-permute-start | bytes 1572872 | tf_op jit(solution)/shard_map/while/body/eval_jaxpr/ppermute | solution.py:186
  468.6 26.3 %collective-permute-start.1 = (bf16[4,32,2048]{2,1,0:T(8,128)(2,1)}, bf16[4,32,2048]{2,1,0:T(8,128)(2,1)S(1)}, u32[]{:S(2)}, u32[]{:S(2)}) collective-permute-start(bf16[4,32,2048]{2,1,0:T(8,128)(2,1)} %get-tuple-element.682), channel_id=1, source_target_pairs={{32,0},{64,32},{96,64},{128,96},{160,128},{192,160},{224,192},{33,... | collective-permute-start | bytes 1572872 | tf_op jit(solution)/shard_map/while/body/eval_jaxpr/ppermute | solution.py:186
  499.3 10.7 %collective-permute-start.1 = (bf16[4,32,2048]{2,1,0:T(8,128)(2,1)}, bf16[4,32,2048]{2,1,0:T(8,128)(2,1)S(1)}, u32[]{:S(2)}, u32[]{:S(2)}) collective-permute-start(bf16[4,32,2048]{2,1,0:T(8,128)(2,1)} %get-tuple-element.682), channel_id=1, source_target_pairs={{32,0},{64,32},{96,64},{128,96},{160,128},{192,160},{224,192},{33,... | collective-permute-start | bytes 1572872 | tf_op jit(solution)/shard_map/while/body/eval_jaxpr/ppermute | solution.py:186
  514.4 15.4 %collective-permute-start.1 = (bf16[4,32,2048]{2,1,0:T(8,128)(2,1)}, bf16[4,32,2048]{2,1,0:T(8,128)(2,1)S(1)}, u32[]{:S(2)}, u32[]{:S(2)}) collective-permute-start(bf16[4,32,2048]{2,1,0:T(8,128)(2,1)} %get-tuple-element.682), channel_id=1, source_target_pairs={{32,0},{64,32},{96,64},{128,96},{160,128},{192,160},{224,192},{33,... | collective-permute-start | bytes 1572872 | tf_op jit(solution)/shard_map/while/body/eval_jaxpr/ppermute | solution.py:186
  534.2 298.5 %collective-permute-start.1 = (bf16[4,32,2048]{2,1,0:T(8,128)(2,1)}, bf16[4,32,2048]{2,1,0:T(8,128)(2,1)S(1)}, u32[]{:S(2)}, u32[]{:S(2)}) collective-permute-start(bf16[4,32,2048]{2,1,0:T(8,128)(2,1)} %get-tuple-element.682), channel_id=1, source_target_pairs={{32,0},{64,32},{96,64},{128,96},{160,128},{192,160},{224,192},{33,... | collective-permute-start | bytes 1572872 | tf_op jit(solution)/shard_map/while/body/eval_jaxpr/ppermute | solution.py:186
  841.4 6.6 copy-start.2
  841.4 6.6 copy-start.4
  869.1 5.8 copy-start
  869.1 5.8 copy-start.6
  879.4 4.0 collective-permute-start.1
  (25 other events, 53.8 us)
Sparse Core Ops, SparseCore 0:
  10.6 87.3 all-gather.8
  100.5 78.5 all-gather.10
  181.7 74.8 all-gather.6
where the time goes:
time: 967 us; the launch traced here: 964 us
  waiting for transfers between devices  579 us (60%)
  starting transfers between devices  129 us (13%)
  blocking collectives  73.4 us (8%)
  local copies, waits for them, and re-layouts  59.4 us (6%)
  other arithmetic  54 us (6%)
  matrix products  39.5 us (4%)
  loops' own time  16.4 us (2%)
  between operations  14 us (1%)
    ppermute x8, waiting for transfers between devices, backward_step(): sent = lax.ppermute(grad_in, 'section', backward_route)  371 us
    ppermute x8, starting transfers between devices, forward_step(): sent = lax.ppermute(hidden_new, 'section', forward_route)  108 us
    all_gather x1, waiting for transfers between devices, body(): lax.all_gather(w_out[0], 'dp', axis=1, tiled=True)  74.7 us
    psum x1, blocking collectives, body(): total = lax.psum(grad_sum, 'dp')  73.4 us
    all_gather x1, waiting for transfers between devices, body(): lax.all_gather(w_keyval[0], 'dp', axis=0, tiled=True)  71 us
    all_gather x1, waiting for transfers between devices, body(): lax.all_gather(w_query[0], 'dp', axis=0, tiled=True)  32.7 us
    all_to_all x1, waiting for transfers between devices, body(): lax.all_to_all(packed, 'dp', split_axis=0, concat_axis=0, tiled=True)  26.9 us
  transfers between devices with their start and end apart: 20, of which 13 were waited for; matrix products, arithmetic and copies ran while one was open for 6% of the time, Pallas kernels for 0%

commit v1 on v0

--- a/solution.py
+++ b/solution.py
@@ -191,7 +191,7 @@
         (zero_block, jnp.zeros_like(steering)),
         jnp.arange(section_count - 1, -1, -1, dtype=jnp.int32),
     )
-    total = lax.psum(grad_sum, "dp")
+    total = jnp.sum(lax.all_gather(grad_sum, "dp"), axis=0)
     return (produced[None], total[None])
 
 

time: 967 us -> 942 us (0.974)
  blocking collectives: 73.4 us -> 47.8 us
    psum x1 -> x0, blocking collectives: 73.4 us -> none  [body(): total = lax.psum(grad_sum, 'dp')]
    all_gather x0 -> x1, blocking collectives: none -> 47.8 us  [body(): total = jnp.sum(lax.all_gather(grad_sum, 'dp'), axis=0)]
where the time goes in v1:
time: 942 us; the launch traced here: 939 us
  waiting for transfers between devices  579 us (61%)
  starting transfers between devices  129 us (14%)
  local copies, waits for them, and re-layouts  59.4 us (6%)
  other arithmetic  54.6 us (6%)
  blocking collectives  47.8 us (5%)
  matrix products  39.5 us (4%)
  loops' own time  16.4 us (2%)
  between operations  14 us (1%)
    ppermute x8, waiting for transfers between devices, backward_step(): sent = lax.ppermute(grad_in, 'section', backward_route)  371 us
    ppermute x8, starting transfers between devices, forward_step(): sent = lax.ppermute(hidden_new, 'section', forward_route)  108 us
    all_gather x1, waiting for transfers between devices, body(): lax.all_gather(w_out[0], 'dp', axis=1, tiled=True)  74.7 us
    all_gather x1, waiting for transfers between devices, body(): lax.all_gather(w_keyval[0], 'dp', axis=0, tiled=True)  71 us
    all_gather x1, blocking collectives, body(): total = jnp.sum(lax.all_gather(grad_sum, 'dp'), axis=0)  47.8 us
    all_gather x1, waiting for transfers between devices, body(): lax.all_gather(w_query[0], 'dp', axis=0, tiled=True)  32.7 us
    all_to_all x1, waiting for transfers between devices, body(): lax.all_to_all(packed, 'dp', split_axis=0, concat_axis=0, tiled=True)  26.9 us
  transfers between devices with their start and end apart: 20, of which 13 were waited for; matrix products, arithmetic and copies ran while one was open for 6% of the time, Pallas kernels for 0%

profile of v1, /device:TPU:0, one launch (start us, length us, event | category | flops | bytes accessed | tf_op | source)
XLA Modules:
  0.0 939.2 jit_solution(15473372592379680056)
XLA Ops:
  21.3 10.0 %all-to-all-start = ((bf16[32,4,2,2048]{3,2,1,0:T(2,128)(2,1)}), bf16[32,4,2,2048]{3,2,1,0:T(2,128)(2,1)S(1)}, u32[]{:S(2)}, u32[]{:S(2)}) async-start(bf16[32,4,2,2048]{3,2,1,0:T(2,128)(2,1)} %pad_maximum_fusion.3), calls=%async_computation | async-start | bytes 2097152 | tf_op jit(solution)/shard_map/all_to_all | solution.py:139
  36.0 26.9 %all-to-all-done = bf16[32,4,2,2048]{3,2,1,0:T(2,128)(2,1)S(1)} async-done(((bf16[32,4,2,2048]{3,2,1,0:T(2,128)(2,1)}), bf16[32,4,2,2048]{3,2,1,0:T(2,128)(2,1)S(1)}, u32[]{:S(2)}, u32[]{:S(2)}) %all-to-all-start) | async-done | bytes 1048608 | tf_op jit(solution)/shard_map/all_to_all | solution.py:139
  65.2 32.7 %all-gather.10.cloned.1.call-done = bf16[1,2048,1024]{2,1,0:T(8,128)(2,1)} async-done(((bf16[1,64,1024]{2,1,0:T(8,128)(2,1)}), bf16[1,2048,1024]{2,1,0:T(8,128)(2,1)}) %all-gather.10.cloned.1.call-update) | async-done | bytes 4194320 | tf_op jit(solution)/shard_map/all_gather | solution.py:120
  104.4 74.7 %all-gather.12.cloned.1.call-done = bf16[1,1024,2048]{1,2,0:T(8,128)(2,1)} async-done(((bf16[1,1024,64]{1,2,0:T(8,128)(2,1)}), bf16[1,1024,2048]{1,2,0:T(8,128)(2,1)}) %all-gather.12.cloned.1.call-update) | async-done | bytes 4194320 | tf_op jit(solution)/shard_map/all_gather | solution.py:122
  179.1 6.5 copy.80
  185.6 71.0 %all-gather.8.cloned.1.call-done = bf16[1,2048,512]{2,1,0:T(8,128)(2,1)} async-done(((bf16[1,64,512]{2,1,0:T(8,128)(2,1)}), bf16[1,2048,512]{2,1,0:T(8,128)(2,1)}) %all-gather.8.cloned.1.call-update) | async-done | bytes 2097168 | tf_op jit(solution)/shard_map/all_gather | solution.py:121
  256.7 157.6 %while.28 = (s32[]{:T(128)}, bf16[4,32,2048]{2,1,0:T(8,128)(2,1)S(1)}, bf16[4,32,2048]{2,1,0:T(8,128)(2,1)S(1)}, bf16[4,32,2048]{2,1,0:T(8,128)(2,1)}, s32[8]{0:...) while((s32[]{:T(128)}, ...), condition=%wide.region_14.15_spmd.clone, body=%wide.region_8.14_spmd.clone.sunk | while | flops 1376075008 | bytes 24693816 | solution.py:168
  258.7 18.0 %conditional.6 = (bf16[4,32,2048]{2,1,0:T(8,128)(2,1)S(1)}) conditional(s32[]{:T(128)} %convert_element_type.335, () %tuple.113, (bf16[4,32,2048]{2,1,0:T(8,128)(2,1)S(1)}, f32[1,2048]{1,0:T(1,128)}, f32[1,2048]{1,0:T(1,128)}, bf16[2048,512]{1,0:T(8,128)(2,1)}, s32[4,32]{1,0:T(4,128)}, /*index=5*/s32[4,32]{1,0:T(4,128)}, ...), branch_computations={%region_9.9_spmd, %region_10.13_spmd} | conditional | flops 1374764288 | bytes 18402056 | solution.py:163
  281.5 20.2 %collective-permute-start = (bf16[4,32,2048]{2,1,0:T(8,128)(2,1)S(1)}, bf16[4,32,2048]{2,1,0:T(8,128)(2,1)S(1)}, u32[]{:S(2)}, u32[]{:S(2)}) collective-permute-start(bf16[4,32,2048]{2,1,0:T(8,128)(2,1)S(1)} %get-tuple-element.784), channel_id=1, source_target_pairs={{0,32},{32,64},{64,96},{96,128},{128,160},{160,192},{192,224},{1,3... | collective-permute-start | bytes 1572872 | tf_op jit(solution)/shard_map/while/body/eval_jaxpr/ppermute | solution.py:165
  315.8 26.5 %collective-permute-start = (bf16[4,32,2048]{2,1,0:T(8,128)(2,1)S(1)}, bf16[4,32,2048]{2,1,0:T(8,128)(2,1)S(1)}, u32[]{:S(2)}, u32[]{:S(2)}) collective-permute-start(bf16[4,32,2048]{2,1,0:T(8,128)(2,1)S(1)} %get-tuple-element.784), channel_id=1, source_target_pairs={{0,32},{32,64},{64,96},{96,128},{128,160},{160,192},{192,224},{1,3... | collective-permute-start | bytes 1572872 | tf_op jit(solution)/shard_map/while/body/eval_jaxpr/ppermute | solution.py:165
  346.2 8.6 collective-permute-start
  358.7 13.1 %collective-permute-start = (bf16[4,32,2048]{2,1,0:T(8,128)(2,1)S(1)}, bf16[4,32,2048]{2,1,0:T(8,128)(2,1)S(1)}, u32[]{:S(2)}, u32[]{:S(2)}) collective-permute-start(bf16[4,32,2048]{2,1,0:T(8,128)(2,1)S(1)} %get-tuple-element.784), channel_id=1, source_target_pairs={{0,32},{32,64},{64,96},{96,128},{128,160},{160,192},{192,224},{1,3... | collective-permute-start | bytes 1572872 | tf_op jit(solution)/shard_map/while/body/eval_jaxpr/ppermute | solution.py:165
  375.8 8.6 collective-permute-start
  388.3 24.0 %collective-permute-start = (bf16[4,32,2048]{2,1,0:T(8,128)(2,1)S(1)}, bf16[4,32,2048]{2,1,0:T(8,128)(2,1)S(1)}, u32[]{:S(2)}, u32[]{:S(2)}) collective-permute-start(bf16[4,32,2048]{2,1,0:T(8,128)(2,1)S(1)} %get-tuple-element.784), channel_id=1, source_target_pairs={{0,32},{32,64},{64,96},{96,128},{128,160},{160,192},{192,224},{1,3... | collective-permute-start | bytes 1572872 | tf_op jit(solution)/shard_map/while/body/eval_jaxpr/ppermute | solution.py:165
  415.2 469.1 %while.29 = (s32[]{:T(128)}, bf16[4,32,2048]{2,1,0:T(8,128)(2,1)}, f32[2048]{0:T(1024)}, s32[8]{0:T(128)}, s32[]{:T(128)}, /*index=5*/bf16[4,32,2048]{2,1,0:T(8,...) while((s32[]{:T(128)}, bf16[4,32,2048]{2,1,0:T(8,128)(2,1)}, ...), condition=%wide.region_26.27_spmd.clone, body=%wide.region_15.26_spmd.clone.sunk | while | flops 2205098752 | bytes 54051516 | solution.py:189
  421.3 7.6 collective-permute-done.1
  435.8 13.3 %collective-permute-done.1 = bf16[4,32,2048]{2,1,0:T(8,128)(2,1)S(1)} collective-permute-done((bf16[4,32,2048]{2,1,0:T(8,128)(2,1)}, bf16[4,32,2048]{2,1,0:T(8,128)(2,1)S(1)}, u32[]{:S(2)}, u32[]{:S(2)}) %collective-permute-start.1) | collective-permute-done | bytes 524320 | tf_op jit(solution)/shard_map/while/body/eval_jaxpr/ppermute | solution.py:186
  456.2 8.1 collective-permute-done.1
  471.2 23.7 %collective-permute-done.1 = bf16[4,32,2048]{2,1,0:T(8,128)(2,1)S(1)} collective-permute-done((bf16[4,32,2048]{2,1,0:T(8,128)(2,1)}, bf16[4,32,2048]{2,1,0:T(8,128)(2,1)S(1)}, u32[]{:S(2)}, u32[]{:S(2)}) %collective-permute-start.1) | collective-permute-done | bytes 524320 | tf_op jit(solution)/shard_map/while/body/eval_jaxpr/ppermute | solution.py:186
  502.0 8.1 collective-permute-done.1
  517.0 12.8 %collective-permute-done.1 = bf16[4,32,2048]{2,1,0:T(8,128)(2,1)S(1)} collective-permute-done((bf16[4,32,2048]{2,1,0:T(8,128)(2,1)}, bf16[4,32,2048]{2,1,0:T(8,128)(2,1)S(1)}, u32[]{:S(2)}, u32[]{:S(2)}) %collective-permute-start.1) | collective-permute-done | bytes 524320 | tf_op jit(solution)/shard_map/while/body/eval_jaxpr/ppermute | solution.py:186
  536.9 295.9 %collective-permute-done.1 = bf16[4,32,2048]{2,1,0:T(8,128)(2,1)S(1)} collective-permute-done((bf16[4,32,2048]{2,1,0:T(8,128)(2,1)}, bf16[4,32,2048]{2,1,0:T(8,128)(2,1)S(1)}, u32[]{:S(2)}, u32[]{:S(2)}) %collective-permute-start.1) | collective-permute-done | bytes 524320 | tf_op jit(solution)/shard_map/while/body/eval_jaxpr/ppermute | solution.py:186
  835.7 43.7 %conditional.7 = (bf16[4,32,2048]{2,1,0:T(8,128)(2,1)}, f32[2048]{0:T(1024)}) conditional(s32[]{:T(128)} %convert_element_type.336, () %tuple.116, (s32[]{:T(128)}, bf16[4,32,2048]{2,1,0:T(8,128)(2,1)}, bf16[4,32,2048]{2,1,0:T(8,128)(2,1)}, bf16[1024,2048]{1,0:T(8,128)(2,1)}, s32[4,32]{1,0:T(4,128)}, ...), branch_computations={%region_16.16_spmd, %region_17.25_spmd} | conditional | flops 2205094656 | bytes 49832296 | solution.py:183
  884.3 47.8 %all-gather.3 = f32[65536]{0:T(1024)S(1)} all-gather(f32[2048]{0:T(1024)} %get-tuple-element.237), channel_id=5, replica_groups=mesh['section'=8,'dp'=32] {'dp'}, dimensions={0}, use_global_device_ids=true | all-gather | bytes 270336 | tf_op jit(solution)/shard_map/all_gather | solution.py:194
  (279 shorter events, 179.9 us)
Async XLA Ops:
  7.2 90.8 %all-gather.10.cloned.1.call-start = ((), (), s32[]{:S(2)}) async-start(), calls=%async_computation.2 | async-start | bytes 4325376 | tf_op jit(solution)/shard_map/all_gather | solution.py:120
  7.9 171.2 %all-gather.12.cloned.1.call-start = ((), (), s32[]{:S(2)}) async-start(), calls=%async_computation.3 | async-start | bytes 4325376 | tf_op jit(solution)/shard_map/all_gather | solution.py:122
  8.6 248.0 %all-gather.8.cloned.1.call-start = ((), (), s32[]{:S(2)}) async-start(), calls=%async_computation.1 | async-start | bytes 2162688 | tf_op jit(solution)/shard_map/all_gather | solution.py:121
  21.3 41.6 %all-to-all-start = ((bf16[32,4,2,2048]{3,2,1,0:T(2,128)(2,1)}), bf16[32,4,2,2048]{3,2,1,0:T(2,128)(2,1)S(1)}, u32[]{:S(2)}, u32[]{:S(2)}) async-start(bf16[32,4,2,2048]{3,2,1,0:T(2,128)(2,1)} %pad_maximum_fusion.3), calls=%async_computation | async-start | bytes 2097152 | tf_op jit(solution)/shard_map/all_to_all | solution.py:139
  276.6 2.8 collective-permute-start
  281.5 22.1 %collective-permute-start = (bf16[4,32,2048]{2,1,0:T(8,128)(2,1)S(1)}, bf16[4,32,2048]{2,1,0:T(8,128)(2,1)S(1)}, u32[]{:S(2)}, u32[]{:S(2)}) collective-permute-start(bf16[4,32,2048]{2,1,0:T(8,128)(2,1)S(1)} %get-tuple-element.784), channel_id=1, source_target_pairs={{0,32},{32,64},{64,96},{96,128},{128,160},{160,192},{192,224},{1,3... | collective-permute-start | bytes 1572872 | tf_op jit(solution)/shard_map/while/body/eval_jaxpr/ppermute | solution.py:165
  305.7 8.0 collective-permute-start
  315.8 28.4 %collective-permute-start = (bf16[4,32,2048]{2,1,0:T(8,128)(2,1)S(1)}, bf16[4,32,2048]{2,1,0:T(8,128)(2,1)S(1)}, u32[]{:S(2)}, u32[]{:S(2)}) collective-permute-start(bf16[4,32,2048]{2,1,0:T(8,128)(2,1)S(1)} %get-tuple-element.784), channel_id=1, source_target_pairs={{0,32},{32,64},{64,96},{96,128},{128,160},{160,192},{192,224},{1,3... | collective-permute-start | bytes 1572872 | tf_op jit(solution)/shard_map/while/body/eval_jaxpr/ppermute | solution.py:165
  346.2 10.5 %collective-permute-start = (bf16[4,32,2048]{2,1,0:T(8,128)(2,1)S(1)}, bf16[4,32,2048]{2,1,0:T(8,128)(2,1)S(1)}, u32[]{:S(2)}, u32[]{:S(2)}) collective-permute-start(bf16[4,32,2048]{2,1,0:T(8,128)(2,1)S(1)} %get-tuple-element.784), channel_id=1, source_target_pairs={{0,32},{32,64},{64,96},{96,128},{128,160},{160,192},{192,224},{1,3... | collective-permute-start | bytes 1572872 | tf_op jit(solution)/shard_map/while/body/eval_jaxpr/ppermute | solution.py:165
  358.7 15.0 %collective-permute-start = (bf16[4,32,2048]{2,1,0:T(8,128)(2,1)S(1)}, bf16[4,32,2048]{2,1,0:T(8,128)(2,1)S(1)}, u32[]{:S(2)}, u32[]{:S(2)}) collective-permute-start(bf16[4,32,2048]{2,1,0:T(8,128)(2,1)S(1)} %get-tuple-element.784), channel_id=1, source_target_pairs={{0,32},{32,64},{64,96},{96,128},{128,160},{160,192},{192,224},{1,3... | collective-permute-start | bytes 1572872 | tf_op jit(solution)/shard_map/while/body/eval_jaxpr/ppermute | solution.py:165
  375.8 10.5 %collective-permute-start = (bf16[4,32,2048]{2,1,0:T(8,128)(2,1)S(1)}, bf16[4,32,2048]{2,1,0:T(8,128)(2,1)S(1)}, u32[]{:S(2)}, u32[]{:S(2)}) collective-permute-start(bf16[4,32,2048]{2,1,0:T(8,128)(2,1)S(1)} %get-tuple-element.784), channel_id=1, source_target_pairs={{0,32},{32,64},{64,96},{96,128},{128,160},{160,192},{192,224},{1,3... | collective-permute-start | bytes 1572872 | tf_op jit(solution)/shard_map/while/body/eval_jaxpr/ppermute | solution.py:165
  388.3 25.9 %collective-permute-start = (bf16[4,32,2048]{2,1,0:T(8,128)(2,1)S(1)}, bf16[4,32,2048]{2,1,0:T(8,128)(2,1)S(1)}, u32[]{:S(2)}, u32[]{:S(2)}) collective-permute-start(bf16[4,32,2048]{2,1,0:T(8,128)(2,1)S(1)} %get-tuple-element.784), channel_id=1, source_target_pairs={{0,32},{32,64},{64,96},{96,128},{128,160},{160,192},{192,224},{1,3... | collective-permute-start | bytes 1572872 | tf_op jit(solution)/shard_map/while/body/eval_jaxpr/ppermute | solution.py:165
  418.7 10.2 %collective-permute-start.1 = (bf16[4,32,2048]{2,1,0:T(8,128)(2,1)}, bf16[4,32,2048]{2,1,0:T(8,128)(2,1)S(1)}, u32[]{:S(2)}, u32[]{:S(2)}) collective-permute-start(bf16[4,32,2048]{2,1,0:T(8,128)(2,1)} %get-tuple-element.682), channel_id=1, source_target_pairs={{32,0},{64,32},{96,64},{128,96},{160,128},{192,160},{224,192},{33,... | collective-permute-start | bytes 1572872 | tf_op jit(solution)/shard_map/while/body/eval_jaxpr/ppermute | solution.py:186
  433.2 15.9 %collective-permute-start.1 = (bf16[4,32,2048]{2,1,0:T(8,128)(2,1)}, bf16[4,32,2048]{2,1,0:T(8,128)(2,1)S(1)}, u32[]{:S(2)}, u32[]{:S(2)}) collective-permute-start(bf16[4,32,2048]{2,1,0:T(8,128)(2,1)} %get-tuple-element.682), channel_id=1, source_target_pairs={{32,0},{64,32},{96,64},{128,96},{160,128},{192,160},{224,192},{33,... | collective-permute-start | bytes 1572872 | tf_op jit(solution)/shard_map/while/body/eval_jaxpr/ppermute | solution.py:186
  453.6 10.7 %collective-permute-start.1 = (bf16[4,32,2048]{2,1,0:T(8,128)(2,1)}, bf16[4,32,2048]{2,1,0:T(8,128)(2,1)S(1)}, u32[]{:S(2)}, u32[]{:S(2)}) collective-permute-start(bf16[4,32,2048]{2,1,0:T(8,128)(2,1)} %get-tuple-element.682), channel_id=1, source_target_pairs={{32,0},{64,32},{96,64},{128,96},{160,128},{192,160},{224,192},{33,... | collective-permute-start | bytes 1572872 | tf_op jit(solution)/shard_map/while/body/eval_jaxpr/ppermute | solution.py:186
  468.6 26.3 %collective-permute-start.1 = (bf16[4,32,2048]{2,1,0:T(8,128)(2,1)}, bf16[4,32,2048]{2,1,0:T(8,128)(2,1)S(1)}, u32[]{:S(2)}, u32[]{:S(2)}) collective-permute-start(bf16[4,32,2048]{2,1,0:T(8,128)(2,1)} %get-tuple-element.682), channel_id=1, source_target_pairs={{32,0},{64,32},{96,64},{128,96},{160,128},{192,160},{224,192},{33,... | collective-permute-start | bytes 1572872 | tf_op jit(solution)/shard_map/while/body/eval_jaxpr/ppermute | solution.py:186
  499.3 10.7 %collective-permute-start.1 = (bf16[4,32,2048]{2,1,0:T(8,128)(2,1)}, bf16[4,32,2048]{2,1,0:T(8,128)(2,1)S(1)}, u32[]{:S(2)}, u32[]{:S(2)}) collective-permute-start(bf16[4,32,2048]{2,1,0:T(8,128)(2,1)} %get-tuple-element.682), channel_id=1, source_target_pairs={{32,0},{64,32},{96,64},{128,96},{160,128},{192,160},{224,192},{33,... | collective-permute-start | bytes 1572872 | tf_op jit(solution)/shard_map/while/body/eval_jaxpr/ppermute | solution.py:186
  514.4 15.4 %collective-permute-start.1 = (bf16[4,32,2048]{2,1,0:T(8,128)(2,1)}, bf16[4,32,2048]{2,1,0:T(8,128)(2,1)S(1)}, u32[]{:S(2)}, u32[]{:S(2)}) collective-permute-start(bf16[4,32,2048]{2,1,0:T(8,128)(2,1)} %get-tuple-element.682), channel_id=1, source_target_pairs={{32,0},{64,32},{96,64},{128,96},{160,128},{192,160},{224,192},{33,... | collective-permute-start | bytes 1572872 | tf_op jit(solution)/shard_map/while/body/eval_jaxpr/ppermute | solution.py:186
  534.2 298.5 %collective-permute-start.1 = (bf16[4,32,2048]{2,1,0:T(8,128)(2,1)}, bf16[4,32,2048]{2,1,0:T(8,128)(2,1)S(1)}, u32[]{:S(2)}, u32[]{:S(2)}) collective-permute-start(bf16[4,32,2048]{2,1,0:T(8,128)(2,1)} %get-tuple-element.682), channel_id=1, source_target_pairs={{32,0},{64,32},{96,64},{128,96},{160,128},{192,160},{224,192},{33,... | collective-permute-start | bytes 1572872 | tf_op jit(solution)/shard_map/while/body/eval_jaxpr/ppermute | solution.py:186
  841.4 6.6 copy-start.2
  841.4 6.6 copy-start.4
  869.1 5.8 copy-start
  869.1 5.8 copy-start.6
  879.4 4.0 collective-permute-start.1
  (25 other events, 53.8 us)
Sparse Core Ops, SparseCore 0:
  10.6 87.3 all-gather.9
  100.5 78.5 all-gather.11
  181.7 74.8 all-gather.7
